TPU v7x, 128 devices: a whole 4x4x4 slice. The times are simulated.
128 devices in a mesh: cfg: 2 (over core), row: 4 (over z), col: 16 (over y, x).
Axes of the slice: x: 4, y: 4, z: 4, core: 2. Of those that a mesh axis runs over, the one named last changes fastest.
Arguments:
- img_tokens: bfloat16 [2, 16, 1024, 3072], P('cfg', 'col', None, 'row'), may hold values from -6 to 6
- txt_tokens: bfloat16 [2, 16, 512, 3072], P('cfg', 'col', None, 'row'), may hold values from -6 to 6
- img_mod: bfloat16 [2, 16, 2, 3072], P('cfg', 'col', None, 'row'), may hold values from -3 to 3
- txt_mod: bfloat16 [2, 16, 2, 3072], P('cfg', 'col', None, 'row'), may hold values from -3 to 3
- img_gate: bfloat16 [2, 16, 3072], P('cfg', 'col', 'row'), may hold values from -16 to 16
- txt_len: int32 [2, 16], P('cfg', 'col'), may hold values from 128 to 512, as said below
- img_qkv_weight: bfloat16 [3072, 3, 3072], P('col', None, 'row'), may hold values from -0.109375 to 0.109375
- txt_kv_weight: bfloat16 [3072, 2, 3072], P('col', None, 'row'), may hold values from -0.109375 to 0.109375
- out_weight: bfloat16 [3072, 3072], P('row', 'col'), may hold values from -0.109375 to 0.109375
- final_weight: bfloat16 [3072, 64], P('row'), may hold values from -0.109375 to 0.109375
- latent: float32 [16, 1024, 64], P('col', ('cfg', 'row')), may hold values from -6 to 6
- sigmas: float32 [5], replicated, may hold values from 0 to 2, as said below
- step_index: int32 [1], replicated, may hold values from 0 to 3
- guidance: float32 [1], replicated, may hold values from 1.5 to 5
Outputs:
- img_out: bfloat16 [2, 16, 1024, 3072], P('cfg', 'col', None, 'row')
- latent_next: float32 [16, 1024, 64], P('col', ('cfg', 'row'))
Inputs may be any that keep to these rules, and one draw needn't show every extreme that they name: `txt_len`: in each half some prompt has all 512 text slots live and some other prompt exactly 128. `sigmas`: falls strictly along the table.
All inputs are finite; a program needn't handle non-finite values.
Results may differ from a plain program's by a relative error of at most 0.015.
Values may be sent and summed in bfloat16 or wider, within the bound.
No kernel may reach another device: no remote copies, remote signals or barrier semaphores. Data moves between devices by JAX's collectives and lax.ppermute only.
A program may use at most 128 MiB of HBM per device.

v0:
```python
import math
import jax
import jax.numpy as jnp
from jax import lax
from jax.sharding import PartitionSpec as P

HD = 128


def modulate(tokens, shift_scale):
    values = tokens.astype(jnp.float32)
    centre = values - jnp.mean(values, -1, keepdims=True)
    spread = jnp.mean(centre * centre, -1, keepdims=True)
    normed = centre * lax.rsqrt(spread + 1e-06)
    scaled = normed * (1.0 + shift_scale[..., 1:2, :].astype(jnp.float32))
    return (scaled + shift_scale[..., 0:1, :].astype(jnp.float32)).astype(jnp.bfloat16)


def rms_norm(values):
    return values * lax.rsqrt(jnp.mean(values * values, -1, keepdims=True) + 1e-06)


def add_rows(piece, ready):
    return jnp.dot(ready, piece.reshape(piece.shape[0], -1), preferred_element_type=jnp.float32)


def shards(
    img_tokens,
    txt_tokens,
    img_mod,
    txt_mod,
    img_gate,
    txt_len,
    img_qkv_weight,
    txt_kv_weight,
    out_weight,
    final_weight,
    latent,
    sigmas,
    step_index,
    guidance,
):
    img_whole, txt_whole, img_shift, txt_shift = (
        lax.all_gather(img_tokens, "row", axis=3, tiled=True),
        lax.all_gather(txt_tokens, "row", axis=3, tiled=True),
        lax.all_gather(img_mod, "row", axis=3, tiled=True),
        lax.all_gather(txt_mod, "row", axis=3, tiled=True),
    )
    prompts = img_tokens.shape[1]
    images = img_tokens.shape[2]
    text_slots = txt_tokens.shape[2]
    local_width = img_qkv_weight.shape[2]
    heads_here = local_width // HD
    img_ready = modulate(img_whole[0], img_shift[0]).reshape(prompts * images, -1)
    txt_ready = modulate(txt_whole[0], txt_shift[0]).reshape(prompts * text_slots, -1)
    img_proj = add_rows(lax.all_gather(img_qkv_weight, "col", axis=0, tiled=True), img_ready)
    txt_proj = add_rows(lax.all_gather(txt_kv_weight, "col", axis=0, tiled=True), txt_ready)
    img_proj = img_proj.reshape(prompts, images, 3, heads_here, HD)
    txt_proj = txt_proj.reshape(prompts, text_slots, 2, heads_here, HD)
    queries = rms_norm(img_proj[:, :, 0]).astype(jnp.bfloat16)
    key_rows = jnp.concatenate(
        [rms_norm(txt_proj[:, :, 0]), rms_norm(img_proj[:, :, 1])], 1
    ).astype(jnp.bfloat16)
    value_rows = jnp.concatenate([txt_proj[:, :, 1], img_proj[:, :, 2]], 1).astype(jnp.bfloat16)
    positions = jnp.arange(text_slots + images, dtype=jnp.int32)
    scores = jnp.einsum(
        "qhe,khe->hqk", queries[0], key_rows[0], preferred_element_type=jnp.float32
    ) / math.sqrt(HD)
    usable = (positions < txt_len[0, 0]) | (positions >= text_slots)
    weights = jnp.where(usable, jnp.exp(scores), 0.0)
    chances = (weights / jnp.sum(weights, -1, keepdims=True)).astype(jnp.bfloat16)
    mixed = jnp.einsum("hqk,khe->qhe", chances, value_rows[0], preferred_element_type=jnp.float32)
    outputs = mixed.reshape(images, local_width).astype(jnp.bfloat16)
    head_terms = jnp.dot(
        outputs,
        lax.all_gather(out_weight, "col", axis=1, tiled=True),
        preferred_element_type=jnp.float32,
    )
    projected = (
        lax.psum_scatter(head_terms.astype(jnp.bfloat16), "row", scatter_dimension=1, tiled=True)
        .astype(jnp.float32)
        .reshape(prompts, images, local_width)
    )
    gating = img_gate[0][:, None, :].astype(jnp.float32)
    img_out = (img_tokens[0].astype(jnp.float32) + gating * projected).astype(jnp.bfloat16)
    velocity = jnp.dot(
        img_out.reshape(prompts * images, local_width),
        final_weight,
        preferred_element_type=jnp.float32,
    )
    velocity = velocity.reshape(prompts, images, -1)
    strength = guidance[0]
    share = jnp.where(lax.axis_index("cfg") == 1, strength, 1.0 - strength)
    weighted = velocity * share
    halved = lax.psum_scatter(weighted.astype(jnp.bfloat16), "cfg", scatter_dimension=1, tiled=True)
    guided = lax.psum_scatter(halved, "row", scatter_dimension=1, tiled=True).astype(jnp.float32)
    position_now = step_index[0]
    step_size = sigmas[position_now + 1] - sigmas[position_now]
    return (img_out[None], latent + step_size * guided)


def solution(mesh):
    return jax.shard_map(
        shards,
        mesh=mesh,
        in_specs=(
            P("cfg", "col", None, "row"),
            P("cfg", "col", None, "row"),
            P("cfg", "col", None, "row"),
            P("cfg", "col", None, "row"),
            P("cfg", "col", "row"),
            P("cfg", "col"),
            P("col", None, "row"),
            P("col", None, "row"),
            P("row", "col"),
            P("row", None),
            P("col", ("cfg", "row"), None),
            P(),
            P(),
            P(),
        ),
        out_specs=(P("cfg", "col", None, "row"), P("col", ("cfg", "row"), None)),
        check_vma=False,
    )
```

profile of v0, /device:TPU:0, one launch (start us, length us, event | category | flops | bytes accessed | tf_op | source)
XLA Modules:
  0.0 494.2 jit_solution(1742859976843953743)
XLA Ops:
  10.6 13.4 %all_gather.25 = bf16[1,1,2,3072]{3,2,1,0:T(2,128)(2,1)S(1)} all-gather(bf16[1,1,2,768]{3,2,1,0:T(2,128)(2,1)} %param.16), channel_id=1, replica_groups=mesh['cfg'=2,'row'=4,'col'=16] {'row'}, dimensions={3}, use_global_device_ids=true | all-gather | bytes 15360 | tf_op jit(solution)/shard_map/all_gather | solution.py:46
  24.0 12.4 %all_gather.22 = bf16[1,1,2,3072]{3,2,1,0:T(2,128)(2,1)S(1)} all-gather(bf16[1,1,2,768]{3,2,1,0:T(2,128)(2,1)} %param.17), channel_id=1, replica_groups=mesh['cfg'=2,'row'=4,'col'=16] {'row'}, dimensions={3}, use_global_device_ids=true | all-gather | bytes 15360 | tf_op jit(solution)/shard_map/all_gather | solution.py:47
  37.2 14.8 %all-gather.6.cloned.1.call-done = bf16[1,1,512,3072]{3,2,1,0:T(8,128)(2,1)} async-done(((bf16[1,1,512,768]{3,2,1,0:T(8,128)(2,1)}), bf16[1,1,512,3072]{3,2,1,0:T(8,128)(2,1)}) %all-gather.6.cloned.1.call-update) | async-done | bytes 3145744 | tf_op jit(solution)/shard_map/all_gather | solution.py:45
  52.0 2.5 convert_reduce_fusion.1
  55.8 63.7 %all-gather.10.cloned.1.call-done = bf16[1,1,1024,3072]{3,2,1,0:T(8,128)(2,1)} async-done(((bf16[1,1,1024,768]{3,2,1,0:T(8,128)(2,1)}), bf16[1,1,1024,3072]{3,2,1,0:T(8,128)(2,1)}) %all-gather.10.cloned.1.call-update) | async-done | bytes 6291472 | tf_op jit(solution)/shard_map/all_gather | solution.py:44
  119.5 3.8 convert_reduce_fusion
  124.1 1.8 fusion.8
  125.9 71.7 %all-gather.8.cloned.1.call-done = bf16[3072,2,768]{2,1,0:T(2,128)(2,1)} async-done(((bf16[192,2,768]{2,1,0:T(2,128)(2,1)}), bf16[3072,2,768]{2,1,0:T(2,128)(2,1)}) %all-gather.8.cloned.1.call-update) | async-done | bytes 9437200 | tf_op jit(solution)/shard_map/all_gather | solution.py:57
  197.6 23.8 %copy.27 = bf16[3072,2,768]{0,2,1:T(8,128)(2,1)} copy(bf16[3072,2,768]{2,1,0:T(2,128)(2,1)} %all-gather.8.cloned.1.call-done) | data formatting | bytes 18874368 | tf_op jit(solution)/shard_map/reshape | solution.py:24
  221.4 8.5 %fusion.43 = f32[1,512,2,6,128]{4,1,3,2,0:T(8,128)S(1)} fusion(bf16[2,6,128,3072]{3,2,1,0:T(8,128)(2,1)} %bitcast.111, bf16[1,1,512,3072]{3,2,1,0:T(8,128)(2,1)S(1)} %copy-done.3, f32[3072]{0:T(1024)S(1)} %bitcast.121, f32[3072]{0:T(1024)S(1)} %bitcast.120, f32[512]{0:T(512)S(1)} %add_rsqrt_fusion.4, f32[512]{0:T(512)S(1)} %broadcast_multiply_fusion.1), kind=kOutput, calls=%fused_computation.54 | convolution fusion | flops 4841275392 | bytes 15757312 | tf_op jit(solution)/shard_map/dot_general | solution.py:24
  231.4 1.4 fusion.51
  232.7 64.3 %all-gather.12.cloned.1.call-done = bf16[3072,3,768]{2,0,1:T(8,128)(2,1)} async-done(((bf16[192,3,768]{2,0,1:T(8,128)(2,1)}), bf16[3072,3,768]{2,0,1:T(8,128)(2,1)}) %all-gather.12.cloned.1.call-update) | async-done | bytes 14155792 | tf_op jit(solution)/shard_map/all_gather | solution.py:56
  297.0 18.7 %copy.22 = bf16[3072,3,768]{0,2,1:T(8,128)(2,1)} copy(bf16[3072,3,768]{2,0,1:T(8,128)(2,1)} %all-gather.12.cloned.1.call-done) | data formatting | bytes 28311552 | tf_op jit(solution)/shard_map/all_gather | solution.py:56
  315.7 21.6 %fusion.23 = f32[1,1024,3,6,128]{4,1,3,2,0:T(8,128)S(1)} fusion(bf16[3,6,128,3072]{3,2,1,0:T(8,128)(2,1)} %bitcast.110, bf16[1,1,1024,3072]{3,2,1,0:T(8,128)(2,1)} %all-gather.10.cloned.1.call-done, f32[3072]{0:T(1024)S(1)} %bitcast.119, f32[3072]{0:T(1024)S(1)} %bitcast.118, f32[1024]{0:T(1024)S(1)} %add_rsqrt_fusion.3, f32[1024]{0:T(1024)S(1)} %broadcast_multiply_fusion), kind=kOutput, calls=%fused_computation.31 | convolution fusion | flops 14514388992 | bytes 29917184 | tf_op jit(solution)/shard_map/dot_general | solution.py:24
  337.4 1.7 multiply_reduce_fusion.1
  341.2 18.4 %fusion = (f32[6,1024]{1,0:T(8,128)S(1)}, f32[6,1024,1536]{2,1,0:T(8,128)}) fusion(pred[1536]{0:T(1024)(128)(4,1)S(1)} %fusion.60, bf16[1024,6,128]{2,0,1:T(8,128)(2,1)S(1)} %fusion.30, bf16[512,6,128]{2,0,1:T(8,128)(2,1)} %fusion.51, f32[1,1024,3,6,128]{4,1,3,2,0:T(8,128)} %copy-done.2, f32[1024,6]{0,1:T(8,128)S(1)} %get-tuple-element.9), kind=kOutput, calls=%fused_computation.2 | convolution fusion | flops 2450515968 | bytes 43304448 | tf_op jit(solution)/shard_map/qhe,khe->hqk/dot_general | solution.py:66
  359.5 15.2 %fusion.46 = bf16[6,128,1024]{2,1,0:T(8,128)(2,1)S(1)} fusion(f32[6,1024,1536]{2,1,0:T(8,128)} %get-tuple-element.7, f32[6,1024]{1,0:T(8,128)S(1)} %get-tuple-element.6, pred[1536]{0:T(1024)(128)(4,1)S(1)} %fusion.60, bf16[1024,6,128]{2,0,1:T(8,128)(2,1)S(1)} %fusion.50, bf16[512,6,128]{2,0,1:T(8,128)(2,1)} %fusion.55), kind=kOutput, calls=%fused_computation.55 | convolution fusion | flops 2459172864 | bytes 41707008 | tf_op jit(solution)/shard_map/hqk,khe->qhe/dot_general | solution.py:72
  374.8 9.4 %convolution_convert_fusion = bf16[1024,3072]{1,0:T(8,128)(2,1)} fusion(bf16[1024,768]{0,1:T(8,128)(2,1)S(1)} %bitcast.122, bf16[768,3072]{0,1:T(8,128)(2,1)} %all-gather.14.cloned.1.call-done), kind=kOutput, calls=%fused_computation.30 | convolution fusion | flops 4834983936 | bytes 12582912 | tf_op jit(solution)/shard_map/dot_general | solution.py:74
  385.1 63.3 %reduce-scatter.6.cloned.1.call-done = bf16[1024,768]{1,0:T(8,128)(2,1)} async-done(((bf16[1024,3072]{1,0:T(8,128)(2,1)}), bf16[1024,768]{1,0:T(8,128)(2,1)}) %reduce-scatter.6.cloned.1.call-update) | async-done | bytes 1572880 | tf_op jit(solution)/shard_map/reduce_scatter | solution.py:80
  448.4 2.9 fusion.54
  453.8 7.3 %reduce-scatter.8.cloned.1.call-done = bf16[1,512,64]{1,2,0:T(8,128)(2,1)} async-done(((bf16[1,1024,64]{1,2,0:T(8,128)(2,1)}), bf16[1,512,64]{1,2,0:T(8,128)(2,1)}) %reduce-scatter.8.cloned.1.call-update) | async-done | bytes 65552 | tf_op jit(solution)/shard_map/reduce_scatter | solution.py:95
  461.1 1.0 copy.28
  462.8 1.6 fusion.57
  464.4 21.4 %reduce-scatter.10.cloned.1.call-done = bf16[128,64]{1,0:T(8,128)(2,1)} async-done(((bf16[512,64]{1,0:T(8,128)(2,1)}), bf16[128,64]{1,0:T(8,128)(2,1)}) %reduce-scatter.10.cloned.1.call-update) | async-done | bytes 16400
  (57 shorter events, 12.0 us)
Async XLA Ops:
  7.2 441.2 %copy-start = (bf16[768,64]{0,1:T(8,128)(2,1)S(1)}, bf16[768,64]{0,1:T(8,128)(2,1)}, u32[]{:S(2)}) copy-start(bf16[768,64]{0,1:T(8,128)(2,1)} %param.23) | copy-start | bytes 294916
  7.2 44.8 %all-gather.6.cloned.1.call-start = ((), (), s32[]{:S(2)}) async-start(), calls=%async_computation.3 | async-start | bytes 3932160 | tf_op jit(solution)/shard_map/all_gather | solution.py:45
  7.9 111.6 %all-gather.10.cloned.1.call-start = ((), (), s32[]{:S(2)}) async-start(), calls=%async_computation.5 | async-start | bytes 7864320 | tf_op jit(solution)/shard_map/all_gather | solution.py:44
  8.7 188.9 %all-gather.8.cloned.1.call-start = ((), (), s32[]{:S(2)}) async-start(), calls=%async_computation.4 | async-start | bytes 10027008 | tf_op jit(solution)/shard_map/all_gather | solution.py:57
  9.4 287.6 %all-gather.12.cloned.1.call-start = ((), (), s32[]{:S(2)}) async-start(), calls=%async_computation.6 | async-start | bytes 15040512 | tf_op jit(solution)/shard_map/all_gather | solution.py:56
  10.0 364.8 %all-gather.14.cloned.1.call-start = ((), (), s32[]{:S(2)}) async-start(), calls=%async_computation.7 | async-start | bytes 5013504 | tf_op jit(solution)/shard_map/all_gather | solution.py:76
  10.6 437.8 %reduce-scatter.6.cloned.1.call-start = ((), (), s32[]{:S(2)}) async-start(), calls=%async_computation.8 | async-start | bytes 7864320 | tf_op jit(solution)/shard_map/reduce_scatter | solution.py:80
  52.0 2.8 copy-start.3
  119.5 4.6 copy-start.1
  337.3 3.6 copy-start.2
  384.2 0.8 copy-start.7
  384.2 64.1 %copy-start.4 = (bf16[1,1,1024,768]{3,2,1,0:T(8,128)(2,1)S(1)}, bf16[1,1,1024,768]{3,2,1,0:T(8,128)(2,1)}, u32[]{:S(2)}) copy-start(bf16[1,1,1024,768]{3,2,1,0:T(8,128)(2,1)} %param.14) | copy-start | bytes 4718596
  384.2 67.7 %copy-start.8 = (f32[5]{0:T(128)S(1)}, f32[5]{0:T(128)}, u32[]{:S(2)}) copy-start(f32[5]{0:T(128)} %param.25) | copy-start | bytes 64
  384.2 76.8 %reduce-scatter.8.cloned.1.call-start = ((), (), s32[]{:S(2)}) async-start(), calls=%async_computation.9 | async-start | bytes 196608 | tf_op jit(solution)/shard_map/reduce_scatter | solution.py:95
  385.1 101.6 %copy-start.6 = (f32[1,128,64]{1,2,0:T(8,128)S(1)}, f32[1,128,64]{1,2,0:T(8,128)}, u32[]{:S(2)}) copy-start(f32[1,128,64]{1,2,0:T(8,128)} %param.24) | copy-start | bytes 98308
  448.4 14.4 %copy-start.5 = (bf16[1024,768]{1,0:T(8,128)(2,1)S(1)}, bf16[1024,768]{1,0:T(8,128)(2,1)}, u32[]{:S(2)}) copy-start(bf16[1024,768]{1,0:T(8,128)(2,1)} %reduce-scatter.6.cloned.1.call-done) | copy-start | bytes 4718596
  451.2 34.6 %reduce-scatter.10.cloned.1.call-start = ((), (), s32[]{:S(2)}) async-start(), calls=%async_computation.10 | async-start | bytes 163840
Sparse Core Ops, SparseCore 0:
  9.6 42.2 all-gather.5
  53.6 65.8 all-gather.9
  121.7 75.8 all-gather.7
  199.6 97.3 all-gather.11
  299.0 53.3 all-gather.13
  384.4 63.9 reduce-scatter.5
  451.4 9.6 reduce-scatter.7
  463.4 22.3 reduce-scatter.9
where the time goes:
time: 496 us; the launch traced here: 494 us
  waiting for transfers between devices  310 us (62%)
  matrix products  76 us (15%)
  local copies, waits for them, and re-layouts  48.8 us (10%)
  blocking collectives  25.8 us (5%)
  between operations  17.6 us (4%)
  other arithmetic  15.9 us (3%)
    all_gather x1, waiting for transfers between devices, shards(): lax.all_gather(txt_kv_weight, 'col', axis=0, tiled=True)  71.7 us
    all_gather x1, waiting for transfers between devices, shards(): lax.all_gather(img_qkv_weight, 'col', axis=0, tiled=True)  64.3 us
    all_gather x1, waiting for transfers between devices, shards(): lax.all_gather(img_tokens, 'row', axis=3, tiled=True)  63.7 us
    reduce_scatter x1, waiting for transfers between devices, shards(): lax.psum_scatter(head_terms.astype(jnp.bfloat16), 'row', scatter_dimensio...  63.3 us
    dot_general x2, matrix products, add_rows(): jnp.dot(ready, piece.reshape(piece.shape[0], -1), preferred_element_type=...  30.1 us
    unnamed x9, waiting for transfers between devices  24.6 us
    reshape x1, local copies, waits for them, and re-layouts, add_rows(): piece.reshape(piece.shape[0], -1)  23.8 us
    all_gather x1, local copies, waits for them, and re-layouts, shards(): lax.all_gather(img_qkv_weight, 'col', axis=0, tiled=True)  18.7 us
  transfers between devices with their start and end apart: 8, of which 7 were waited for; matrix products, arithmetic and copies ran while one was open for 25% of the time, Pallas kernels for 0%

commit v1 on v0

--- a/solution.py
+++ b/solution.py
@@ -43,7 +43,9 @@
     img_whole, txt_whole, img_shift, txt_shift = (
         lax.all_gather(img_tokens, "row", axis=3, tiled=True),
         lax.all_gather(txt_tokens, "row", axis=3, tiled=True),
-        lax.all_gather(img_mod, "row", axis=3, tiled=True),
+        jnp.concatenate(
+            jax.lax.all_to_all(jnp.stack([img_mod] * jax.lax.axis_size("row")), "row", 0, 0), 3
+        ),
         lax.all_gather(txt_mod, "row", axis=3, tiled=True),
     )
     prompts = img_tokens.shape[1]

time: 496 us -> 496 us (level)
  blocking collectives: 25.8 us -> 13 us
  waiting for transfers between devices: 310 us -> 316 us
  starting transfers between devices: 0.31 us -> 5.69 us
    all_gather x1 -> x0, blocking collectives: 13.4 us -> none  [shards(): lax.all_gather(img_mod, 'row', axis=3, tiled=True)]
    all_gather x1, waiting for transfers between devices: 14.8 us -> 20.8 us  [shards(): lax.all_gather(txt_tokens, 'row', axis=3, tiled=True)]
    all_to_all x0 -> x1, starting transfers between devices: none -> 5.42 us  [shards(): jax.lax.all_to_all(jnp.stack([img_mod] * jax.lax.axis_size('row')), 'row'...]
  transfers between devices with their start and end apart: 8 -> 9, of which waited for: 7 -> 7; matrix products, arithmetic and copies ran while one was open for 25% -> 25% of each run, Pallas kernels for 0% -> 0%
where the time goes in v1:
time: 496 us; the launch traced here: 494 us
  waiting for transfers between devices  316 us (64%)
  matrix products  76 us (15%)
  local copies, waits for them, and re-layouts  50.2 us (10%)
  between operations  17.6 us (4%)
  other arithmetic  15.9 us (3%)
  blocking collectives  13 us (3%)
  starting transfers between devices  5.69 us (1%)
    all_gather x1, waiting for transfers between devices, shards(): lax.all_gather(txt_kv_weight, 'col', axis=0, tiled=True)  71.7 us
    all_gather x1, waiting for transfers between devices, shards(): lax.all_gather(img_qkv_weight, 'col', axis=0, tiled=True)  64.2 us
    all_gather x1, waiting for transfers between devices, shards(): lax.all_gather(img_tokens, 'row', axis=3, tiled=True)  63.7 us
    reduce_scatter x1, waiting for transfers between devices, shards(): lax.psum_scatter(head_terms.astype(jnp.bfloat16), 'row', scatter_dimensio...  63.3 us
    dot_general x2, matrix products, add_rows(): jnp.dot(ready, piece.reshape(piece.shape[0], -1), preferred_element_type=...  30.1 us
    unnamed x9, waiting for transfers between devices  24.7 us
    reshape x1, local copies, waits for them, and re-layouts, add_rows(): piece.reshape(piece.shape[0], -1)  23.9 us
    all_gather x1, waiting for transfers between devices, shards(): lax.all_gather(txt_tokens, 'row', axis=3, tiled=True)  20.8 us
  transfers between devices with their start and end apart: 9, of which 7 were waited for; matrix products, arithmetic and copies ran while one was open for 25% of the time, Pallas kernels for 0%

profile of v1, /device:TPU:0, one launch (start us, length us, event | category | flops | bytes accessed | tf_op | source)
XLA Modules:
  0.0 494.2 jit_solution(11897025679552153372)
XLA Ops:
  10.0 1.3 stack.2
  11.3 5.4 %all-to-all-start = ((bf16[4,1,1,2,768]{4,3,2,1,0:T(2,128)(2,1)}), bf16[4,1,1,2,768]{4,3,2,1,0:T(2,128)(2,1)S(1)}, u32[]{:S(2)}, u32[]{:S(2)}) async-start(bf16[4,1,1,2,768]{4,3,2,1,0:T(2,128)(2,1)} %stack.2), calls=%async_computation | async-start | bytes 24576 | tf_op jit(solution)/shard_map/all_to_all | solution.py:47
  17.3 13.0 %all_gather.19 = bf16[1,1,2,3072]{3,2,1,0:T(2,128)(2,1)S(1)} all-gather(bf16[1,1,2,768]{3,2,1,0:T(2,128)(2,1)} %param.17), channel_id=1, replica_groups=mesh['cfg'=2,'row'=4,'col'=16] {'row'}, dimensions={3}, use_global_device_ids=true | all-gather | bytes 15360 | tf_op jit(solution)/shard_map/all_gather | solution.py:49
  31.1 20.8 %all-gather.6.cloned.1.call-done = bf16[1,1,512,3072]{3,2,1,0:T(8,128)(2,1)} async-done(((bf16[1,1,512,768]{3,2,1,0:T(8,128)(2,1)}), bf16[1,1,512,3072]{3,2,1,0:T(8,128)(2,1)}) %all-gather.6.cloned.1.call-update) | async-done | bytes 3145744 | tf_op jit(solution)/shard_map/all_gather | solution.py:45
  51.9 2.5 convert_reduce_fusion.1
  55.7 63.7 %all-gather.10.cloned.1.call-done = bf16[1,1,1024,3072]{3,2,1,0:T(8,128)(2,1)} async-done(((bf16[1,1,1024,768]{3,2,1,0:T(8,128)(2,1)}), bf16[1,1,1024,3072]{3,2,1,0:T(8,128)(2,1)}) %all-gather.10.cloned.1.call-update) | async-done | bytes 6291472 | tf_op jit(solution)/shard_map/all_gather | solution.py:44
  119.5 3.8 convert_reduce_fusion
  124.1 1.8 fusion.8
  125.9 71.7 %all-gather.8.cloned.1.call-done = bf16[3072,2,768]{2,1,0:T(2,128)(2,1)} async-done(((bf16[192,2,768]{2,1,0:T(2,128)(2,1)}), bf16[3072,2,768]{2,1,0:T(2,128)(2,1)}) %all-gather.8.cloned.1.call-update) | async-done | bytes 9437200 | tf_op jit(solution)/shard_map/all_gather | solution.py:59
  197.6 23.9 %copy.27 = bf16[3072,2,768]{0,2,1:T(8,128)(2,1)} copy(bf16[3072,2,768]{2,1,0:T(2,128)(2,1)} %all-gather.8.cloned.1.call-done) | data formatting | bytes 18874368 | tf_op jit(solution)/shard_map/reshape | solution.py:24
  221.4 8.5 %fusion.43 = f32[1,512,2,6,128]{4,1,3,2,0:T(8,128)S(1)} fusion(bf16[2,6,128,3072]{3,2,1,0:T(8,128)(2,1)} %bitcast.114, bf16[1,1,512,3072]{3,2,1,0:T(8,128)(2,1)S(1)} %copy-done.3, f32[3072]{0:T(1024)S(1)} %bitcast.124, f32[3072]{0:T(1024)S(1)} %bitcast.123, f32[512]{0:T(512)S(1)} %add_rsqrt_fusion.4, f32[512]{0:T(512)S(1)} %broadcast_multiply_fusion.1), kind=kOutput, calls=%fused_computation.54 | convolution fusion | flops 4841275392 | bytes 15757312 | tf_op jit(solution)/shard_map/dot_general | solution.py:24
  231.4 1.4 fusion.51
  232.8 64.2 %all-gather.12.cloned.1.call-done = bf16[3072,3,768]{2,0,1:T(8,128)(2,1)} async-done(((bf16[192,3,768]{2,0,1:T(8,128)(2,1)}), bf16[3072,3,768]{2,0,1:T(8,128)(2,1)}) %all-gather.12.cloned.1.call-update) | async-done | bytes 14155792 | tf_op jit(solution)/shard_map/all_gather | solution.py:58
  297.0 18.7 %copy.22 = bf16[3072,3,768]{0,2,1:T(8,128)(2,1)} copy(bf16[3072,3,768]{2,0,1:T(8,128)(2,1)} %all-gather.12.cloned.1.call-done) | data formatting | bytes 28311552 | tf_op jit(solution)/shard_map/all_gather | solution.py:58
  315.7 21.6 %fusion.23 = f32[1,1024,3,6,128]{4,1,3,2,0:T(8,128)S(1)} fusion(bf16[3,6,128,3072]{3,2,1,0:T(8,128)(2,1)} %bitcast.113, bf16[1,1,1024,3072]{3,2,1,0:T(8,128)(2,1)} %all-gather.10.cloned.1.call-done, f32[3072]{0:T(1024)S(1)} %bitcast.122, f32[3072]{0:T(1024)S(1)} %bitcast.121, f32[1024]{0:T(1024)S(1)} %add_rsqrt_fusion.3, f32[1024]{0:T(1024)S(1)} %broadcast_multiply_fusion), kind=kOutput, calls=%fused_computation.31 | convolution fusion | flops 14514388992 | bytes 29917184 | tf_op jit(solution)/shard_map/dot_general | solution.py:24
  337.3 1.7 multiply_reduce_fusion.1
  341.1 18.4 %fusion = (f32[6,1024]{1,0:T(8,128)S(1)}, f32[6,1024,1536]{2,1,0:T(8,128)}) fusion(pred[1536]{0:T(1024)(128)(4,1)S(1)} %fusion.60, bf16[1024,6,128]{2,0,1:T(8,128)(2,1)S(1)} %fusion.30, bf16[512,6,128]{2,0,1:T(8,128)(2,1)} %fusion.51, f32[1,1024,3,6,128]{4,1,3,2,0:T(8,128)} %copy-done.2, f32[1024,6]{0,1:T(8,128)S(1)} %get-tuple-element.9), kind=kOutput, calls=%fused_computation.2 | convolution fusion | flops 2450515968 | bytes 43304448 | tf_op jit(solution)/shard_map/qhe,khe->hqk/dot_general | solution.py:68
  359.5 15.2 %fusion.46 = bf16[6,128,1024]{2,1,0:T(8,128)(2,1)S(1)} fusion(f32[6,1024,1536]{2,1,0:T(8,128)} %get-tuple-element.7, f32[6,1024]{1,0:T(8,128)S(1)} %get-tuple-element.6, pred[1536]{0:T(1024)(128)(4,1)S(1)} %fusion.60, bf16[1024,6,128]{2,0,1:T(8,128)(2,1)S(1)} %fusion.50, bf16[512,6,128]{2,0,1:T(8,128)(2,1)} %fusion.55), kind=kOutput, calls=%fused_computation.55 | convolution fusion | flops 2459172864 | bytes 41707008 | tf_op jit(solution)/shard_map/hqk,khe->qhe/dot_general | solution.py:74
  374.8 9.4 %convolution_convert_fusion = bf16[1024,3072]{1,0:T(8,128)(2,1)} fusion(bf16[1024,768]{0,1:T(8,128)(2,1)S(1)} %bitcast.126, bf16[768,3072]{0,1:T(8,128)(2,1)} %all-gather.14.cloned.1.call-done), kind=kOutput, calls=%fused_computation.30 | convolution fusion | flops 4834983936 | bytes 12582912 | tf_op jit(solution)/shard_map/dot_general | solution.py:76
  385.1 63.3 %reduce-scatter.6.cloned.1.call-done = bf16[1024,768]{1,0:T(8,128)(2,1)} async-done(((bf16[1024,3072]{1,0:T(8,128)(2,1)}), bf16[1024,768]{1,0:T(8,128)(2,1)}) %reduce-scatter.6.cloned.1.call-update) | async-done | bytes 1572880 | tf_op jit(solution)/shard_map/reduce_scatter | solution.py:82
  448.3 2.8 fusion.54
  453.7 7.3 %reduce-scatter.8.cloned.1.call-done = bf16[1,512,64]{1,2,0:T(8,128)(2,1)} async-done(((bf16[1,1024,64]{1,2,0:T(8,128)(2,1)}), bf16[1,512,64]{1,2,0:T(8,128)(2,1)}) %reduce-scatter.8.cloned.1.call-update) | async-done | bytes 65552 | tf_op jit(solution)/shard_map/reduce_scatter | solution.py:97
  462.7 1.6 fusion.57
  464.3 21.5 %reduce-scatter.10.cloned.1.call-done = bf16[128,64]{1,0:T(8,128)(2,1)} async-done(((bf16[512,64]{1,0:T(8,128)(2,1)}), bf16[128,64]{1,0:T(8,128)(2,1)}) %reduce-scatter.10.cloned.1.call-update) | async-done | bytes 16400
  (59 shorter events, 13.0 us)
Async XLA Ops:
  7.2 441.2 %copy-start = (bf16[768,64]{0,1:T(8,128)(2,1)S(1)}, bf16[768,64]{0,1:T(8,128)(2,1)}, u32[]{:S(2)}) copy-start(bf16[768,64]{0,1:T(8,128)(2,1)} %param.23) | copy-start | bytes 294916
  7.2 44.8 %all-gather.6.cloned.1.call-start = ((), (), s32[]{:S(2)}) async-start(), calls=%async_computation.4 | async-start | bytes 3932160 | tf_op jit(solution)/shard_map/all_gather | solution.py:45
  7.9 111.6 %all-gather.10.cloned.1.call-start = ((), (), s32[]{:S(2)}) async-start(), calls=%async_computation.6 | async-start | bytes 7864320 | tf_op jit(solution)/shard_map/all_gather | solution.py:44
  8.7 188.9 %all-gather.8.cloned.1.call-start = ((), (), s32[]{:S(2)}) async-start(), calls=%async_computation.5 | async-start | bytes 10027008 | tf_op jit(solution)/shard_map/all_gather | solution.py:59
  9.4 287.6 %all-gather.12.cloned.1.call-start = ((), (), s32[]{:S(2)}) async-start(), calls=%async_computation.7 | async-start | bytes 15040512 | tf_op jit(solution)/shard_map/all_gather | solution.py:58
  11.3 19.8 %all-to-all-start = ((bf16[4,1,1,2,768]{4,3,2,1,0:T(2,128)(2,1)}), bf16[4,1,1,2,768]{4,3,2,1,0:T(2,128)(2,1)S(1)}, u32[]{:S(2)}, u32[]{:S(2)}) async-start(bf16[4,1,1,2,768]{4,3,2,1,0:T(2,128)(2,1)} %stack.2), calls=%async_computation | async-start | bytes 24576 | tf_op jit(solution)/shard_map/all_to_all | solution.py:47
  16.7 358.1 %all-gather.14.cloned.1.call-start = ((), (), s32[]{:S(2)}) async-start(), calls=%async_computation.8 | async-start | bytes 5013504 | tf_op jit(solution)/shard_map/all_gather | solution.py:78
  17.3 431.1 %reduce-scatter.6.cloned.1.call-start = ((), (), s32[]{:S(2)}) async-start(), calls=%async_computation.9 | async-start | bytes 7864320 | tf_op jit(solution)/shard_map/reduce_scatter | solution.py:82
  51.9 2.8 copy-start.3
  119.5 4.6 copy-start.1
  337.3 3.6 copy-start.2
  384.2 0.8 copy-start.7
  384.2 64.1 %copy-start.4 = (bf16[1,1,1024,768]{3,2,1,0:T(8,128)(2,1)S(1)}, bf16[1,1,1024,768]{3,2,1,0:T(8,128)(2,1)}, u32[]{:S(2)}) copy-start(bf16[1,1,1024,768]{3,2,1,0:T(8,128)(2,1)} %param.14) | copy-start | bytes 4718596
  384.2 67.7 %copy-start.8 = (f32[5]{0:T(128)S(1)}, f32[5]{0:T(128)}, u32[]{:S(2)}) copy-start(f32[5]{0:T(128)} %param.25) | copy-start | bytes 64
  384.2 76.8 %reduce-scatter.8.cloned.1.call-start = ((), (), s32[]{:S(2)}) async-start(), calls=%async_computation.10 | async-start | bytes 196608 | tf_op jit(solution)/shard_map/reduce_scatter | solution.py:97
  385.0 101.6 %copy-start.6 = (f32[1,128,64]{1,2,0:T(8,128)S(1)}, f32[1,128,64]{1,2,0:T(8,128)}, u32[]{:S(2)}) copy-start(f32[1,128,64]{1,2,0:T(8,128)} %param.24) | copy-start | bytes 98308
  448.3 14.4 %copy-start.5 = (bf16[1024,768]{1,0:T(8,128)(2,1)S(1)}, bf16[1024,768]{1,0:T(8,128)(2,1)}, u32[]{:S(2)}) copy-start(bf16[1024,768]{1,0:T(8,128)(2,1)} %reduce-scatter.6.cloned.1.call-done) | copy-start | bytes 4718596
  451.2 34.6 %reduce-scatter.10.cloned.1.call-start = ((), (), s32[]{:S(2)}) async-start(), calls=%async_computation.11 | async-start | bytes 163840
Sparse Core Ops, SparseCore 0:
  9.6 42.2 all-gather.5
  53.6 65.8 all-gather.9
  121.6 75.8 all-gather.7
  199.6 97.3 all-gather.11
  299.0 53.3 all-gather.13
  384.3 63.9 reduce-scatter.5
  451.3 9.6 reduce-scatter.7
  463.4 22.3 reduce-scatter.9
